TPU v7x, 32 devices: a whole 2x2x4 slice. The times are simulated.
32 devices in a mesh: dp: 4 (over z), expert: 4 (over y, x), tensor: 2 (over core).
Axes of the slice: x: 2, y: 2, z: 4, core: 2. Of those that a mesh axis runs over, the one named last changes fastest.
Arguments:
- tokens: bfloat16 [2048, 2048], P(('dp', 'expert')), may hold values from -6 to 6
- grad_out: bfloat16 [2048, 2048], P(('dp', 'expert')), may hold values from -6 to 6
- route_ids: int32 [2048, 8], P(('dp', 'expert')), may hold values from 0 to 15, all different within a row; in each aligned block of 128 rows (0 to 127, 128 to 255, ...) at most 72 rows name the same one
- gate_values: bfloat16 [2048, 8], P(('dp', 'expert')), may hold values from 0.049804688 to 0.5
- gate_proj: bfloat16 [16, 2048, 768], P(('dp', 'expert'), None, 'tensor'), may hold values from -0.125 to 0.125
- up_proj: bfloat16 [16, 2048, 768], P(('dp', 'expert'), None, 'tensor'), may hold values from -0.125 to 0.125
- down_proj: bfloat16 [16, 768, 2048], P(('dp', 'expert'), 'tensor'), may hold values from -0.21875 to 0.21875
Outputs:
- token_grad: bfloat16 [2048, 2048], P(('dp', 'expert'), 'tensor')
- gate_grad: bfloat16 [2048, 8], P(('dp', 'expert'))
- gate_proj_grad: bfloat16 [16, 2048, 768], P(('dp', 'expert'), None, 'tensor')
- up_proj_grad: bfloat16 [16, 2048, 768], P(('dp', 'expert'), None, 'tensor')
- down_proj_grad: bfloat16 [16, 768, 2048], P(('dp', 'expert'), 'tensor')
Inputs may be any that keep to these rules, and one draw needn't show every extreme that they name: `route_ids`: each token names 8 different experts. Among the rows of one device (128 tokens), no expert is named more than 72 times, a bound that some block reaches.
All inputs are finite; a program needn't handle non-finite values.
Results may differ from a plain program's by a relative error of at most 0.008.
Values may be sent and summed in bfloat16 or wider, within the bound.
No kernel may reach another device: no remote copies, remote signals or barrier semaphores. Data moves between devices by JAX's collectives and lax.ppermute only.
A program may use at most 128 MiB of HBM per device.

v0:
```python
import jax
import jax.numpy as jnp
from jax import lax
from jax.sharding import PartitionSpec as P


def on_device(tokens, grad_out, route_ids, gate_values, gate_proj, up_proj, down_proj):
    tok_rows, features = tokens.shape
    top_count = route_ids.shape[1]
    n_dp = lax.axis_size("dp")
    n_ex = lax.axis_size("expert")
    groups = n_dp * n_ex
    capacity = max(2, tok_rows * top_count * 9 // (8 * groups))
    plane = lax.axis_index("dp")
    core = lax.axis_index("tensor")
    col_rows = n_dp * tok_rows
    plane_slots = n_dp * capacity
    slots = n_ex * plane_slots
    ids_all = lax.all_gather(route_ids, "dp", tiled=True)
    gates_all = lax.all_gather(gate_values, "dp", tiled=True)
    carried = jnp.where(core == 0, tokens, grad_out)
    carried_all = lax.all_gather(carried, "dp", tiled=True)
    routes = tok_rows * top_count
    ids_blk = ids_all.reshape(n_dp, routes)
    local_ex = ids_blk - plane * n_ex
    in_plane = (local_ex >= 0) & (local_ex < n_ex)
    one_hot = local_ex[:, :, None] == jnp.arange(n_ex, dtype=jnp.int32)[None, None, :]
    one_hot_b = one_hot.astype(jnp.bfloat16)
    r_iota = jnp.arange(routes, dtype=jnp.int32)
    earlier = (r_iota[None, :] < r_iota[:, None]).astype(jnp.bfloat16)
    running = jnp.einsum("ab,nbe->nae", earlier, one_hot_b, preferred_element_type=jnp.float32)
    position = jnp.sum(running * one_hot.astype(jnp.float32), axis=2).astype(jnp.int32)
    blk = jnp.arange(n_dp, dtype=jnp.int32)[:, None]
    slot_of = jnp.where(in_plane, local_ex * plane_slots + blk * capacity + position, -1)
    slot_of = slot_of.reshape(col_rows, top_count)
    s_iota = jnp.arange(slots, dtype=jnp.int32)
    match = slot_of[None, :, :] == s_iota[:, None, None]
    select = jnp.sum(match.astype(jnp.bfloat16), axis=2)
    send = jnp.dot(select, carried_all, preferred_element_type=jnp.float32).astype(tokens.dtype)
    send_gate = jnp.sum(
        jnp.where(match, gates_all.astype(jnp.float32)[None, :, :], 0.0), axis=(1, 2)
    ).astype(gate_values.dtype)
    recv = lax.all_to_all(send, "expert", split_axis=0, concat_axis=0, tiled=True)
    routed_gate = lax.all_to_all(send_gate, "expert", split_axis=0, concat_axis=0, tiled=True)
    both = lax.all_gather(recv, "tensor")
    routed_x = both[0]
    routed_dy = both[1]
    weight_g = gate_proj[0]
    weight_u = up_proj[0]
    weight_d = down_proj[0]
    gate_pre = jnp.dot(routed_x, weight_g, preferred_element_type=jnp.float32)
    up_pre = jnp.dot(routed_x, weight_u, preferred_element_type=jnp.float32)
    sig_gate = jax.nn.sigmoid(gate_pre)
    silu_gate = gate_pre * sig_gate
    activation = (silu_gate * up_pre).astype(jnp.bfloat16)
    hidden_grad = lax.dot_general(
        routed_dy, weight_d, (((1,), (1,)), ((), ())), preferred_element_type=jnp.float32
    )
    gate_terms = jnp.sum(hidden_grad * activation.astype(jnp.float32), axis=1)
    row_gate = routed_gate.astype(jnp.float32)[:, None]
    scaled = row_gate * hidden_grad
    up_grad = (scaled * silu_gate).astype(jnp.bfloat16)
    pre_grad = (scaled * up_pre * sig_gate * (1.0 + gate_pre * (1.0 - sig_gate))).astype(
        jnp.bfloat16
    )
    grad_g = lax.dot_general(
        routed_x, pre_grad, (((0,), (0,)), ((), ())), preferred_element_type=jnp.float32
    ).astype(jnp.bfloat16)
    grad_u = lax.dot_general(
        routed_x, up_grad, (((0,), (0,)), ((), ())), preferred_element_type=jnp.float32
    ).astype(jnp.bfloat16)
    weighted = (row_gate * activation.astype(jnp.float32)).astype(jnp.bfloat16)
    grad_d = lax.dot_general(
        weighted, routed_dy, (((0,), (0,)), ((), ())), preferred_element_type=jnp.float32
    ).astype(jnp.bfloat16)
    partial_value = lax.dot_general(
        pre_grad, weight_g, (((1,), (1,)), ((), ())), preferred_element_type=jnp.float32
    ) + lax.dot_general(
        up_grad, weight_u, (((1,), (1,)), ((), ())), preferred_element_type=jnp.float32
    )
    routed_grad = lax.psum_scatter(partial_value, "tensor", scatter_dimension=1, tiled=True).astype(
        jnp.bfloat16
    )
    slot_gate = lax.psum(gate_terms, "tensor").astype(jnp.bfloat16)
    back_rows = lax.all_to_all(routed_grad, "expert", split_axis=0, concat_axis=0, tiled=True)
    back_gate = lax.all_to_all(slot_gate, "expert", split_axis=0, concat_axis=0, tiled=True)
    col_grad = lax.dot_general(
        select, back_rows, (((0,), (0,)), ((), ())), preferred_element_type=jnp.float32
    )
    token_grad = lax.psum_scatter(col_grad, "dp", scatter_dimension=0, tiled=True).astype(
        jnp.bfloat16
    )
    col_gate = jnp.sum(jnp.where(match, back_gate.astype(jnp.float32)[:, None, None], 0.0), axis=0)
    gate_grad = lax.psum_scatter(col_gate, "dp", scatter_dimension=0, tiled=True).astype(
        jnp.bfloat16
    )
    return (token_grad, gate_grad, grad_g[None], grad_u[None], grad_d[None])


def solution(mesh):
    in_specs = (
        P(("dp", "expert"), None),
        P(("dp", "expert"), None),
        P(("dp", "expert"), None),
        P(("dp", "expert"), None),
        P(("dp", "expert"), None, "tensor"),
        P(("dp", "expert"), None, "tensor"),
        P(("dp", "expert"), "tensor", None),
    )
    out_specs = (
        P(("dp", "expert"), "tensor"),
        P(("dp", "expert"), None),
        P(("dp", "expert"), None, "tensor"),
        P(("dp", "expert"), None, "tensor"),
        P(("dp", "expert"), "tensor", None),
    )
    return jax.shard_map(
        on_device, mesh=mesh, in_specs=in_specs, out_specs=out_specs, check_vma=False
    )
```

profile of v0, /device:TPU:0, one launch (start us, length us, event | category | flops | bytes accessed | tf_op | source)
XLA Modules:
  0.0 313.8 jit_solution(6951644346922703783)
XLA Ops:
  9.4 16.3 %all_gather.15 = s32[512,8]{1,0:T(8,128)S(1)} all-gather(s32[128,8]{1,0:T(8,128)S(1)} %copy.20), channel_id=1, replica_groups=mesh['dp'=4,'expert'=4,'tensor'=2] {'dp'}, dimensions={0}, use_global_device_ids=true | all-gather | bytes 20480 | tf_op jit(solution)/shard_map/all_gather | solution.py:19
  26.9 12.2 %fusion.1 = bf16[1152,512]{1,0:T(8,128)(2,1)S(1)} fusion(s32[512,8]{0,1:T(8,128)S(1)} %copy.21), kind=kLoop, calls=%fused_computation.5 | loop fusion | flops 13565952 | bytes 1196032 | tf_op jit(solution)/shard_map/reduce_sum | solution.py:38
  39.1 20.3 %all-gather.3.cloned.1.call-done = bf16[512,2048]{1,0:T(8,128)(2,1)} async-done(((bf16[128,2048]{1,0:T(8,128)(2,1)}), bf16[512,2048]{1,0:T(8,128)(2,1)}) %all-gather.3.cloned.1.call-update) | async-done | bytes 2097168 | tf_op jit(solution)/shard_map/all_gather | solution.py:22
  59.4 4.4 %convolution_convert_fusion = bf16[1152,2048]{1,0:T(8,128)(2,1)S(1)} fusion(bf16[1152,512]{1,0:T(8,128)(2,1)S(1)} %fusion.1, bf16[512,2048]{1,0:T(8,128)(2,1)} %all-gather.3.cloned.1.call-done), kind=kOutput, calls=%fused_computation.6 | convolution fusion | flops 2418278400 | bytes 7995392 | tf_op jit(solution)/shard_map/dot_general | solution.py:39
  63.9 57.6 %all_to_all.37 = bf16[4,288,2048]{2,1,0:T(8,128)(2,1)} all-to-all(bf16[4,288,2048]{2,1,0:T(8,128)(2,1)S(1)} %bitcast.82), channel_id=1, replica_groups=mesh['dp'=4,'expert'=4,'tensor'=2] {'expert'}, dimensions={0} | all-to-all | bytes 9437184 | tf_op jit(solution)/shard_map/all_to_all | solution.py:43
  121.5 18.9 %all-gather.5.cloned.1.call-done = bf16[2,1152,2048]{2,1,0:T(8,128)(2,1)} async-done(((bf16[1,1152,2048]{2,1,0:T(8,128)(2,1)}), bf16[2,1152,2048]{2,1,0:T(8,128)(2,1)}) %all-gather.5.cloned.1.call-update) | async-done | bytes 9437200 | tf_op jit(solution)/shard_map/all_gather | solution.py:45
  140.4 4.8 %fusion.9 = f32[1152,384]{0,1:T(8,128)S(1)} fusion(bf16[2,1152,2048]{2,1,0:T(8,128)(2,1)} %all-gather.5.cloned.1.call-done, bf16[1,2048,384]{2,1,0:T(8,128)(2,1)S(1)} %copy-done), kind=kOutput, calls=%fused_computation.16 | convolution fusion | flops 1811939328 | bytes 8060928 | tf_op jit(solution)/shard_map/dot_general | solution.py:51
  147.9 3.8 %fusion.17 = (f32[1152]{0:T(1024)S(1)}, bf16[1152,384]{0,1:T(8,128)(2,1)}, f32[1152,384]{0,1:T(8,128)}) fusion(f32[1152,384]{0,1:T(8,128)S(1)} %fusion.10, f32[1152,384]{0,1:T(8,128)S(1)} %fusion.9, bf16[1,384,2048]{2,1,0:T(8,128)(2,1)S(1)} %copy-done.12, bf16[2,1152,2048]{2,1,0:T(8,128)(2,1)S(1)} %copy-done.11), kind=kOutput, calls=%fused_computation.26 | convolution fusion | flops 1815919488 | bytes 12489216 | tf_op jit(solution)/shard_map/dot_general | solution.py:56
  156.2 3.9 %all-to-all-start.3 = ((bf16[4,2,144]{2,1,0:T(2,128)(2,1)}), bf16[4,2,144]{2,1,0:T(2,128)(2,1)S(1)}, u32[]{:S(2)}, u32[]{:S(2)}) async-start(bf16[4,2,144]{2,1,0:T(2,128)(2,1)} %reshape.85), calls=%async_computation.5 | async-start | bytes 8192 | tf_op jit(solution)/shard_map/all_to_all | solution.py:86
  160.1 11.9 %all_gather.16 = bf16[512,8]{0,1:T(8,128)(2,1)S(1)} all-gather(bf16[128,8]{0,1:T(8,128)(2,1)S(1)} %copy-done.10), channel_id=1, replica_groups=mesh['dp'=4,'expert'=4,'tensor'=2] {'dp'}, dimensions={0}, use_global_device_ids=true | all-gather | bytes 10240 | tf_op jit(solution)/shard_map/all_gather | solution.py:20
  172.3 11.9 %select_reduce_fusion = (f32[512,8]{0,1:T(8,128)}, bf16[1152]{0:T(1024)(128)(2,1)S(1)}) fusion(f32[1152]{0:T(1024)S(1)} %reshape.81, s32[512,8]{0,1:T(8,128)S(1)} %copy.21, f32[512,8]{0,1:T(8,128)S(1)} %convert_element_type.95), kind=kLoop, calls=%fused_computation | loop fusion | flops 23587712 | bytes 56064 | tf_op jit(solution)/shard_map/reduce_sum | solution.py:93
  185.0 8.6 %all_to_all.38 = bf16[4,2,144]{2,1,0:T(2,128)(2,1)S(1)} all-to-all(bf16[4,2,144]{2,1,0:T(2,128)(2,1)S(1)} %reshape.87), channel_id=1, replica_groups=mesh['dp'=4,'expert'=4,'tensor'=2] {'expert'}, dimensions={0} | all-to-all | bytes 4608 | tf_op jit(solution)/shard_map/all_to_all | solution.py:44
  193.9 3.4 %multiply_convert_fusion.1 = (bf16[1152,384]{0,1:T(8,128)(2,1)S(1)}, bf16[1152,384]{0,1:T(8,128)(2,1)S(1)}) fusion(f32[1152,384]{0,1:T(8,128)} %get-tuple-element.11, f32[1152]{0:T(1024)S(1)} %reshape.80, f32[1152,384]{0,1:T(8,128)} %copy-done.5, f32[1152,384]{0,1:T(8,128)} %copy-done.6), kind=kLoop, calls=%fused_computation.29 | loop fusion | flops 6193152 | bytes 7082496 | tf_op jit(solution)/shard_map/convert_element_type | solution.py:62
  197.3 2.7 fusion.20
  200.0 5.1 %convolution_add_fusion = f32[1152,2048]{1,0:T(8,128)} fusion(f32[1152,2048]{1,0:T(8,128)S(1)} %fusion.20, bf16[1152,384]{0,1:T(8,128)(2,1)S(1)} %get-tuple-element.9, bf16[1,2048,384]{2,1,0:T(8,128)(2,1)S(1)} %copy-done.8), kind=kOutput, calls=%fused_computation.4 | convolution fusion | flops 1814298624 | bytes 21331968 | tf_op jit(solution)/shard_map/dot_general | solution.py:78
  205.2 15.8 %reduce-scatter.4.cloned.1.call-done = f32[1152,1024]{1,0:T(8,128)} async-done(((f32[1152,2048]{1,0:T(8,128)}), f32[1152,1024]{1,0:T(8,128)}) %reduce-scatter.4.cloned.1.call-update) | async-done | bytes 4718608 | tf_op jit(solution)/shard_map/reduce_scatter | solution.py:81
  221.0 4.1 %convert_element_type.103 = bf16[1152,1024]{1,0:T(8,128)(2,1)} convert(f32[1152,1024]{1,0:T(8,128)} %reduce-scatter.4.cloned.1.call-done) | non-fusion elementwise | flops 1179648 | bytes 7077888 | tf_op jit(solution)/shard_map/convert_element_type | solution.py:81
  225.1 4.0 %all-to-all-start.2 = ((bf16[4,288,1024]{2,1,0:T(8,128)(2,1)}), bf16[4,288,1024]{2,1,0:T(8,128)(2,1)S(1)}, u32[]{:S(2)}, u32[]{:S(2)}) async-start(bf16[4,288,1024]{2,1,0:T(8,128)(2,1)} %bitcast.10), calls=%async_computation.3 | async-start | bytes 4718592 | tf_op jit(solution)/shard_map/all_to_all | solution.py:85
  230.0 27.1 %all-to-all-done.2 = bf16[4,288,1024]{2,1,0:T(8,128)(2,1)S(1)} async-done(((bf16[4,288,1024]{2,1,0:T(8,128)(2,1)}), bf16[4,288,1024]{2,1,0:T(8,128)(2,1)S(1)}, u32[]{:S(2)}, u32[]{:S(2)}) %all-to-all-start.2) | async-done | bytes 2359328 | tf_op jit(solution)/shard_map/all_to_all | solution.py:85
  257.1 4.1 %fusion.38 = f32[512,1024]{1,0:T(8,128)} fusion(bf16[1152,512]{1,0:T(8,128)(2,1)} %copy-done.2, bf16[1152,1024]{1,0:T(8,128)(2,1)S(1)} %bitcast.81), kind=kOutput, calls=%fused_computation.52 | convolution fusion | flops 1207959552 | bytes 5636096 | tf_op jit(solution)/shard_map/dot_general | solution.py:87
  262.4 5.8 %fusion.14 = bf16[1,384,2048]{2,1,0:T(8,128)(2,1)} fusion(bf16[2,1152,2048]{2,1,0:T(8,128)(2,1)} %all-gather.5.cloned.1.call-done, bf16[1152,384]{0,1:T(8,128)(2,1)S(1)} %copy-done.13, f32[1152]{0:T(1024)S(1)} %reshape.80), kind=kOutput, calls=%fused_computation.21 | convolution fusion | flops 1814052864 | bytes 7180800 | tf_op jit(solution)/shard_map/dot_general | solution.py:73
  268.2 6.4 %fusion.15 = bf16[1,2048,384]{2,1,0:T(8,128)(2,1)} fusion(bf16[1152,384]{0,1:T(8,128)(2,1)S(1)} %get-tuple-element.9, bf16[2,1152,2048]{2,1,0:T(8,128)(2,1)} %all-gather.5.cloned.1.call-done), kind=kOutput, calls=%fused_computation.22 | convolution fusion | flops 1812725760 | bytes 7176192 | tf_op jit(solution)/shard_map/dot_general | solution.py:69
  274.7 3.9 %fusion.16 = bf16[1,2048,384]{2,1,0:T(8,128)(2,1)} fusion(bf16[1152,384]{0,1:T(8,128)(2,1)S(1)} %copy-done.4, bf16[2,1152,2048]{2,1,0:T(8,128)(2,1)S(1)} %bitcast.86), kind=kOutput, calls=%fused_computation.23 | convolution fusion | flops 1812725760 | bytes 7176192 | tf_op jit(solution)/shard_map/dot_general | solution.py:66
  279.9 25.6 %reduce-scatter.6.cloned.1.call-done = f32[128,1024]{1,0:T(8,128)} async-done(((f32[512,1024]{1,0:T(8,128)}), f32[128,1024]{1,0:T(8,128)}) %reduce-scatter.6.cloned.1.call-update) | async-done | bytes 524304 | tf_op jit(solution)/shard_map/reduce_scatter | solution.py:90
  (76 shorter events, 16.9 us)
Async XLA Ops:
  7.2 133.2 %copy-start = (bf16[1,2048,384]{2,1,0:T(8,128)(2,1)S(1)}, bf16[1,2048,384]{2,1,0:T(8,128)(2,1)}, u32[]{:S(2)}) copy-start(bf16[1,2048,384]{2,1,0:T(8,128)(2,1)} %param.11) | copy-start | bytes 4718596
  7.2 2.1 copy-start.9
  7.2 52.2 %all-gather.3.cloned.1.call-start = ((), (), s32[]{:S(2)}) async-start(), calls=%async_computation.7 | async-start | bytes 2621440 | tf_op jit(solution)/shard_map/all_gather | solution.py:22
  9.3 131.1 %all-gather.5.cloned.1.call-start = ((), (), s32[]{:S(2)}) async-start(), calls=%async_computation.8 | async-start | bytes 14155776 | tf_op jit(solution)/shard_map/all_gather | solution.py:45
  39.1 24.7 %copy-start.2 = (bf16[1152,512]{1,0:T(8,128)(2,1)}, bf16[1152,512]{1,0:T(8,128)(2,1)S(1)}, u32[]{:S(2)}) copy-start(bf16[1152,512]{1,0:T(8,128)(2,1)S(1)} %fusion.1) | copy-start | bytes 3538948
  121.5 23.7 %copy-start.7 = (bf16[1,2048,384]{2,1,0:T(8,128)(2,1)S(1)}, bf16[1,2048,384]{2,1,0:T(8,128)(2,1)}, u32[]{:S(2)}) copy-start(bf16[1,2048,384]{2,1,0:T(8,128)(2,1)} %param.12) | copy-start | bytes 4718596
  140.4 5.1 %copy-start.11 = (bf16[2,1152,2048]{2,1,0:T(8,128)(2,1)S(1)}, bf16[2,1152,2048]{2,1,0:T(8,128)(2,1)}, u32[]{:S(2)}) copy-start(bf16[2,1152,2048]{2,1,0:T(8,128)(2,1)} %all-gather.5.cloned.1.call-done) | copy-start | bytes 28311556
  145.5 2.4 copy-start.5
  145.5 2.4 copy-start.12
  147.9 3.9 %copy-start.6 = (f32[1152,384]{0,1:T(8,128)}, f32[1152,384]{0,1:T(8,128)S(1)}, u32[]{:S(2)}) copy-start(f32[1152,384]{0,1:T(8,128)S(1)} %fusion.10) | copy-start | bytes 5308420
  147.9 12.2 %copy-start.10 = (bf16[128,8]{0,1:T(8,128)(2,1)S(1)}, bf16[128,8]{0,1:T(8,128)(2,1)}, u32[]{:S(2)}) copy-start(bf16[128,8]{0,1:T(8,128)(2,1)} %param.10) | copy-start | bytes 6148
  156.2 15.8 %all-to-all-start.3 = ((bf16[4,2,144]{2,1,0:T(2,128)(2,1)}), bf16[4,2,144]{2,1,0:T(2,128)(2,1)S(1)}, u32[]{:S(2)}, u32[]{:S(2)}) async-start(bf16[4,2,144]{2,1,0:T(2,128)(2,1)} %reshape.85), calls=%async_computation.5 | async-start | bytes 8192 | tf_op jit(solution)/shard_map/all_to_all | solution.py:86
  160.1 60.9 %reduce-scatter.4.cloned.1.call-start = ((), (), s32[]{:S(2)}) async-start(), calls=%async_computation.9 | async-start | bytes 14155776 | tf_op jit(solution)/shard_map/reduce_scatter | solution.py:81
  197.3 2.7 copy-start.3
  197.3 2.7 copy-start.8
  225.1 32.0 %all-to-all-start.2 = ((bf16[4,288,1024]{2,1,0:T(8,128)(2,1)}), bf16[4,288,1024]{2,1,0:T(8,128)(2,1)S(1)}, u32[]{:S(2)}, u32[]{:S(2)}) async-start(bf16[4,288,1024]{2,1,0:T(8,128)(2,1)} %bitcast.10), calls=%async_computation.3 | async-start | bytes 4718592 | tf_op jit(solution)/shard_map/all_to_all | solution.py:85
  229.1 49.5 %reduce-scatter.8.cloned.1.call-start = ((), (), s32[]{:S(2)}) async-start(), calls=%async_computation.11 | async-start | bytes 20480 | tf_op jit(solution)/shard_map/reduce_scatter | solution.py:94
  229.7 75.8 %reduce-scatter.6.cloned.1.call-start = ((), (), s32[]{:S(2)}) async-start(), calls=%async_computation.10 | async-start | bytes 2621440 | tf_op jit(solution)/shard_map/reduce_scatter | solution.py:90
  261.2 1.2 copy-start.13
  262.4 12.3 %slice-start = ((s8[9437184]{0:T(1024)(128)(4,1)}), s8[4194304]{0:T(1024)(128)(4,1)S(1)}, s32[]{:S(2)}) async-start(s8[9437184]{0:T(1024)(128)(4,1)} %bitcast.85), calls=%async_computation.12 | async-start | bytes 8388608
  262.4 12.3 %slice-start.1 = ((s8[9437184]{0:T(1024)(128)(4,1)}), s8[4194304]{0:T(1024)(128)(4,1)S(1)}, s32[]{:S(2)}) async-start(s8[9437184]{0:T(1024)(128)(4,1)} %bitcast.85), calls=%async_computation.13 | async-start | bytes 8388608
  268.2 6.4 %copy-start.4 = (bf16[1152,384]{0,1:T(8,128)(2,1)S(1)}, bf16[1152,384]{0,1:T(8,128)(2,1)}, u32[]{:S(2)}) copy-start(bf16[1152,384]{0,1:T(8,128)(2,1)} %copy-done.3) | copy-start | bytes 2654212
  268.2 6.4 %slice-start.2 = ((s8[9437184]{0:T(1024)(128)(4,1)}), s8[1048576]{0:T(1024)(128)(4,1)S(1)}, s32[]{:S(2)}) async-start(s8[9437184]{0:T(1024)(128)(4,1)} %bitcast.85), calls=%async_computation.14 | async-start | bytes 2097152
  274.7 32.6 %copy-start.1 = (bf16[1,2048,384]{2,1,0:T(8,128)(2,1)S(1)}, bf16[1,2048,384]{2,1,0:T(8,128)(2,1)}, u32[]{:S(2)}) copy-start(bf16[1,2048,384]{2,1,0:T(8,128)(2,1)} %param.11) | copy-start | bytes 4718596
Sparse Core Ops, SparseCore 0:
  10.2 49.2 all-gather.2
  121.6 18.7 all-gather.4
  205.3 15.6 reduce-scatter.3
  232.4 20.2 reduce-scatter.7
  261.4 44.0 reduce-scatter.5
where the time goes:
time: 314 us
  waiting for transfers between devices  108 us (34%)
  blocking collectives  96.9 us (31%)
  matrix products  44 us (14%)
  other arithmetic  38.3 us (12%)
  between operations  14 us (4%)
  starting transfers between devices  8.28 us (3%)
  local copies, waits for them, and re-layouts  3.91 us (1%)
    all_to_all x1, blocking collectives, on_device(): lax.all_to_all(send, 'expert', split_axis=0, concat_axis=0, tiled=True)  57.6 us
    all_to_all x1, waiting for transfers between devices, on_device(): lax.all_to_all(routed_grad, 'expert', split_axis=0, concat_axis=0, tiled=...  27.1 us
    reduce_scatter x1, waiting for transfers between devices, on_device(): lax.psum_scatter(col_grad, 'dp', scatter_dimension=0, tiled=True)  25.6 us
    all_gather x1, waiting for transfers between devices, on_device(): carried_all = lax.all_gather(carried, 'dp', tiled=True)  20.3 us
    all_gather x1, waiting for transfers between devices, on_device(): both = lax.all_gather(recv, 'tensor')  18.9 us
    all_gather x1, blocking collectives, on_device(): ids_all = lax.all_gather(route_ids, 'dp', tiled=True)  16.3 us
    reduce_scatter x1, waiting for transfers between devices, on_device(): lax.psum_scatter(partial_value, 'tensor', scatter_dimension=1, tiled=True)  15.8 us
    reduce_sum x1, other arithmetic, on_device(): select = jnp.sum(match.astype(jnp.bfloat16), axis=2)  12.2 us
  transfers between devices with their start and end apart: 7, of which 5 were waited for; matrix products, arithmetic and copies ran while one was open for 11% of the time, Pallas kernels for 0%

commit v1 on v0

--- a/solution.py
+++ b/solution.py
@@ -17,7 +17,8 @@
     plane_slots = n_dp * capacity
     slots = n_ex * plane_slots
     ids_all = lax.all_gather(route_ids, "dp", tiled=True)
-    gates_all = lax.all_gather(gate_values, "dp", tiled=True)
+    sent = jnp.stack([gate_values] * lax.axis_size("dp"))
+    gates_all = jnp.concatenate(lax.all_to_all(sent, "dp", 0, 0), axis=0)
     carried = jnp.where(core == 0, tokens, grad_out)
     carried_all = lax.all_gather(carried, "dp", tiled=True)
     routes = tok_rows * top_count

time: 314 us -> 307 us (0.978)
  blocking collectives: 96.9 us -> 83.2 us
  starting transfers between devices: 8.28 us -> 11.8 us
    all_gather x1 -> x0, blocking collectives: 11.9 us -> none  [on_device(): gates_all = lax.all_gather(gate_values, 'dp', tiled=True)]
    all_to_all x1, waiting for transfers between devices: 0.01 us -> 4.67 us  [on_device(): lax.all_to_all(slot_gate, 'expert', split_axis=0, concat_axis=0, tiled=True)]
    all_gather x1, waiting for transfers between devices: 18.9 us -> 14.4 us  [on_device(): both = lax.all_gather(recv, 'tensor')]
    all_to_all x0 -> x1, starting transfers between devices: none -> 3.44 us  [on_device(): gates_all = jnp.concatenate(lax.all_to_all(sent, 'dp', 0, 0), axis=0)]
  transfers between devices with their start and end apart: 7 -> 8, of which waited for: 5 -> 6; matrix products, arithmetic and copies ran while one was open for 11% -> 16% of each run, Pallas kernels for 0% -> 0%
where the time goes in v1:
time: 307 us; the launch traced here: 306 us
  waiting for transfers between devices  110 us (36%)
  blocking collectives  83.2 us (27%)
  matrix products  44 us (14%)
  other arithmetic  38.3 us (12%)
  between operations  14 us (5%)
  starting transfers between devices  11.8 us (4%)
  local copies, waits for them, and re-layouts  5.16 us (2%)
    all_to_all x1, blocking collectives, on_device(): lax.all_to_all(send, 'expert', split_axis=0, concat_axis=0, tiled=True)  57.4 us
    all_to_all x1, waiting for transfers between devices, on_device(): lax.all_to_all(routed_grad, 'expert', split_axis=0, concat_axis=0, tiled=...  27.2 us
    reduce_scatter x1, waiting for transfers between devices, on_device(): lax.psum_scatter(col_grad, 'dp', scatter_dimension=0, tiled=True)  25.5 us
    all_gather x1, waiting for transfers between devices, on_device(): carried_all = lax.all_gather(carried, 'dp', tiled=True)  20.3 us
    reduce_scatter x1, waiting for transfers between devices, on_device(): lax.psum_scatter(partial_value, 'tensor', scatter_dimension=1, tiled=True)  17 us
    all_gather x1, blocking collectives, on_device(): ids_all = lax.all_gather(route_ids, 'dp', tiled=True)  16.3 us
    all_gather x1, waiting for transfers between devices, on_device(): both = lax.all_gather(recv, 'tensor')  14.4 us
    reduce_sum x1, other arithmetic, on_device(): select = jnp.sum(match.astype(jnp.bfloat16), axis=2)  12.2 us
  transfers between devices with their start and end apart: 8, of which 6 were waited for; matrix products, arithmetic and copies ran while one was open for 16% of the time, Pallas kernels for 0%

profile of v1, /device:TPU:0, one launch (start us, length us, event | category | flops | bytes accessed | tf_op | source)
XLA Modules:
  0.0 306.1 jit_solution(3420084015989941428)
XLA Ops:
  9.4 16.3 %all_gather.12 = s32[512,8]{1,0:T(8,128)S(1)} all-gather(s32[128,8]{1,0:T(8,128)S(1)} %copy.23), channel_id=1, replica_groups=mesh['dp'=4,'expert'=4,'tensor'=2] {'dp'}, dimensions={0}, use_global_device_ids=true | all-gather | bytes 20480 | tf_op jit(solution)/shard_map/all_gather | solution.py:19
  26.9 12.2 %fusion.1 = bf16[1152,512]{1,0:T(8,128)(2,1)S(1)} fusion(s32[512,8]{0,1:T(8,128)S(1)} %copy.24), kind=kLoop, calls=%fused_computation.5 | loop fusion | flops 13565952 | bytes 1196032 | tf_op jit(solution)/shard_map/reduce_sum | solution.py:39
  39.1 20.3 %all-gather.3.cloned.1.call-done = bf16[512,2048]{1,0:T(8,128)(2,1)} async-done(((bf16[128,2048]{1,0:T(8,128)(2,1)}), bf16[512,2048]{1,0:T(8,128)(2,1)}) %all-gather.3.cloned.1.call-update) | async-done | bytes 2097168 | tf_op jit(solution)/shard_map/all_gather | solution.py:23
  59.4 4.4 %convolution_convert_fusion = bf16[1152,2048]{1,0:T(8,128)(2,1)S(1)} fusion(bf16[1152,512]{1,0:T(8,128)(2,1)S(1)} %fusion.1, bf16[512,2048]{1,0:T(8,128)(2,1)} %all-gather.3.cloned.1.call-done), kind=kOutput, calls=%fused_computation.6 | convolution fusion | flops 2418278400 | bytes 7995392 | tf_op jit(solution)/shard_map/dot_general | solution.py:40
  63.9 57.4 %all_to_all.42 = bf16[4,288,2048]{2,1,0:T(8,128)(2,1)} all-to-all(bf16[4,288,2048]{2,1,0:T(8,128)(2,1)S(1)} %bitcast.85), channel_id=1, replica_groups=mesh['dp'=4,'expert'=4,'tensor'=2] {'expert'}, dimensions={0} | all-to-all | bytes 9437184 | tf_op jit(solution)/shard_map/all_to_all | solution.py:44
  122.6 3.4 %all-to-all-start = ((bf16[4,128,8]{1,2,0:T(8,128)(2,1)}), bf16[4,128,8]{1,2,0:T(8,128)(2,1)S(1)}, u32[]{:S(2)}, u32[]{:S(2)}) async-start(bf16[4,128,8]{1,2,0:T(8,128)(2,1)} %stack.2), calls=%async_computation | async-start | bytes 16384 | tf_op jit(solution)/shard_map/all_to_all | solution.py:21
  126.0 14.4 %all-gather.5.cloned.1.call-done = bf16[2,1152,2048]{2,1,0:T(8,128)(2,1)} async-done(((bf16[1,1152,2048]{2,1,0:T(8,128)(2,1)}), bf16[2,1152,2048]{2,1,0:T(8,128)(2,1)}) %all-gather.5.cloned.1.call-update) | async-done | bytes 9437200 | tf_op jit(solution)/shard_map/all_gather | solution.py:46
  140.4 4.8 %fusion.9 = f32[1152,384]{0,1:T(8,128)S(1)} fusion(bf16[2,1152,2048]{2,1,0:T(8,128)(2,1)} %all-gather.5.cloned.1.call-done, bf16[1,2048,384]{2,1,0:T(8,128)(2,1)S(1)} %copy-done), kind=kOutput, calls=%fused_computation.16 | convolution fusion | flops 1811939328 | bytes 8060928 | tf_op jit(solution)/shard_map/dot_general | solution.py:52
  147.9 3.8 %fusion.17 = (f32[1152]{0:T(1024)S(1)}, bf16[1152,384]{0,1:T(8,128)(2,1)}, f32[1152,384]{0,1:T(8,128)}) fusion(f32[1152,384]{0,1:T(8,128)S(1)} %fusion.10, f32[1152,384]{0,1:T(8,128)S(1)} %fusion.9, bf16[1,384,2048]{2,1,0:T(8,128)(2,1)S(1)} %copy-done.12, bf16[2,1152,2048]{2,1,0:T(8,128)(2,1)S(1)} %copy-done.11), kind=kOutput, calls=%fused_computation.26 | convolution fusion | flops 1815919488 | bytes 12489216 | tf_op jit(solution)/shard_map/dot_general | solution.py:57
  156.2 3.9 %all-to-all-start.4 = ((bf16[4,2,144]{2,1,0:T(2,128)(2,1)}), bf16[4,2,144]{2,1,0:T(2,128)(2,1)S(1)}, u32[]{:S(2)}, u32[]{:S(2)}) async-start(bf16[4,2,144]{2,1,0:T(2,128)(2,1)} %reshape.95), calls=%async_computation.6 | async-start | bytes 8192 | tf_op jit(solution)/shard_map/all_to_all | solution.py:87
  160.1 4.7 %all-to-all-done.4 = bf16[4,2,144]{2,1,0:T(2,128)(2,1)S(1)} async-done(((bf16[4,2,144]{2,1,0:T(2,128)(2,1)}), bf16[4,2,144]{2,1,0:T(2,128)(2,1)S(1)}, u32[]{:S(2)}, u32[]{:S(2)}) %all-to-all-start.4) | async-done | bytes 2336 | tf_op jit(solution)/shard_map/all_to_all | solution.py:87
  165.0 11.9 %select_reduce_fusion = (f32[512,8]{0,1:T(8,128)}, bf16[1152]{0:T(1024)(128)(2,1)S(1)}) fusion(f32[1152]{0:T(1024)S(1)} %reshape.91, s32[512,8]{0,1:T(8,128)S(1)} %copy.24, f32[512,8]{0,1:T(8,128)S(1)} %bitcast_convert_fusion), kind=kLoop, calls=%fused_computation | loop fusion | flops 23587712 | bytes 56064 | tf_op jit(solution)/shard_map/reduce_sum | solution.py:94
  177.8 7.0 %all_to_all.43 = bf16[4,2,144]{2,1,0:T(2,128)(2,1)S(1)} all-to-all(bf16[4,2,144]{2,1,0:T(2,128)(2,1)S(1)} %reshape.97), channel_id=1, replica_groups=mesh['dp'=4,'expert'=4,'tensor'=2] {'expert'}, dimensions={0} | all-to-all | bytes 4608 | tf_op jit(solution)/shard_map/all_to_all | solution.py:45
  185.0 3.4 %multiply_convert_fusion.1 = (bf16[1152,384]{0,1:T(8,128)(2,1)S(1)}, bf16[1152,384]{0,1:T(8,128)(2,1)S(1)}) fusion(f32[1152,384]{0,1:T(8,128)} %get-tuple-element.11, f32[1152]{0:T(1024)S(1)} %reshape.90, f32[1152,384]{0,1:T(8,128)} %copy-done.5, f32[1152,384]{0,1:T(8,128)} %copy-done.6), kind=kLoop, calls=%fused_computation.29 | loop fusion | flops 6193152 | bytes 7082496 | tf_op jit(solution)/shard_map/convert_element_type | solution.py:63
  191.1 5.1 %convolution_add_fusion = f32[1152,2048]{1,0:T(8,128)} fusion(f32[1152,2048]{1,0:T(8,128)S(1)} %fusion.20, bf16[1152,384]{0,1:T(8,128)(2,1)S(1)} %get-tuple-element.9, bf16[1,2048,384]{2,1,0:T(8,128)(2,1)S(1)} %copy-done.8), kind=kOutput, calls=%fused_computation.4 | convolution fusion | flops 1814298624 | bytes 21331968 | tf_op jit(solution)/shard_map/dot_general | solution.py:79
  196.3 17.0 %reduce-scatter.4.cloned.1.call-done = f32[1152,1024]{1,0:T(8,128)} async-done(((f32[1152,2048]{1,0:T(8,128)}), f32[1152,1024]{1,0:T(8,128)}) %reduce-scatter.4.cloned.1.call-update) | async-done | bytes 4718608 | tf_op jit(solution)/shard_map/reduce_scatter | solution.py:82
  213.3 4.1 %convert_element_type.111 = bf16[1152,1024]{1,0:T(8,128)(2,1)} convert(f32[1152,1024]{1,0:T(8,128)} %reduce-scatter.4.cloned.1.call-done) | non-fusion elementwise | flops 1179648 | bytes 7077888 | tf_op jit(solution)/shard_map/convert_element_type | solution.py:82
  217.4 4.0 %all-to-all-start.3 = ((bf16[4,288,1024]{2,1,0:T(8,128)(2,1)}), bf16[4,288,1024]{2,1,0:T(8,128)(2,1)S(1)}, u32[]{:S(2)}, u32[]{:S(2)}) async-start(bf16[4,288,1024]{2,1,0:T(8,128)(2,1)} %bitcast.11), calls=%async_computation.4 | async-start | bytes 4718592 | tf_op jit(solution)/shard_map/all_to_all | solution.py:86
  222.3 27.2 %all-to-all-done.3 = bf16[4,288,1024]{2,1,0:T(8,128)(2,1)S(1)} async-done(((bf16[4,288,1024]{2,1,0:T(8,128)(2,1)}), bf16[4,288,1024]{2,1,0:T(8,128)(2,1)S(1)}, u32[]{:S(2)}, u32[]{:S(2)}) %all-to-all-start.3) | async-done | bytes 2359328 | tf_op jit(solution)/shard_map/all_to_all | solution.py:86
  249.5 4.1 %fusion.38 = f32[512,1024]{1,0:T(8,128)} fusion(bf16[1152,512]{1,0:T(8,128)(2,1)} %copy-done.2, bf16[1152,1024]{1,0:T(8,128)(2,1)S(1)} %bitcast.84), kind=kOutput, calls=%fused_computation.53 | convolution fusion | flops 1207959552 | bytes 5636096 | tf_op jit(solution)/shard_map/dot_general | solution.py:88
  254.7 5.8 %fusion.14 = bf16[1,384,2048]{2,1,0:T(8,128)(2,1)} fusion(bf16[2,1152,2048]{2,1,0:T(8,128)(2,1)} %all-gather.5.cloned.1.call-done, bf16[1152,384]{0,1:T(8,128)(2,1)S(1)} %copy-done.13, f32[1152]{0:T(1024)S(1)} %reshape.90), kind=kOutput, calls=%fused_computation.21 | convolution fusion | flops 1814052864 | bytes 7180800 | tf_op jit(solution)/shard_map/dot_general | solution.py:74
  260.6 6.4 %fusion.15 = bf16[1,2048,384]{2,1,0:T(8,128)(2,1)} fusion(bf16[1152,384]{0,1:T(8,128)(2,1)S(1)} %get-tuple-element.9, bf16[2,1152,2048]{2,1,0:T(8,128)(2,1)} %all-gather.5.cloned.1.call-done), kind=kOutput, calls=%fused_computation.22 | convolution fusion | flops 1812725760 | bytes 7176192 | tf_op jit(solution)/shard_map/dot_general | solution.py:70
  267.0 3.9 %fusion.16 = bf16[1,2048,384]{2,1,0:T(8,128)(2,1)} fusion(bf16[1152,384]{0,1:T(8,128)(2,1)S(1)} %copy-done.4, bf16[2,1152,2048]{2,1,0:T(8,128)(2,1)S(1)} %bitcast.89), kind=kOutput, calls=%fused_computation.23 | convolution fusion | flops 1812725760 | bytes 7176192 | tf_op jit(solution)/shard_map/dot_general | solution.py:67
  272.2 25.5 %reduce-scatter.6.cloned.1.call-done = f32[128,1024]{1,0:T(8,128)} async-done(((f32[512,1024]{1,0:T(8,128)}), f32[128,1024]{1,0:T(8,128)}) %reduce-scatter.6.cloned.1.call-update) | async-done | bytes 524304 | tf_op jit(solution)/shard_map/reduce_scatter | solution.py:91
  (78 shorter events, 20.8 us)
Async XLA Ops:
  7.2 133.3 %copy-start = (bf16[1,2048,384]{2,1,0:T(8,128)(2,1)S(1)}, bf16[1,2048,384]{2,1,0:T(8,128)(2,1)}, u32[]{:S(2)}) copy-start(bf16[1,2048,384]{2,1,0:T(8,128)(2,1)} %param.11) | copy-start | bytes 4718596
  7.2 2.1 copy-start.9
  7.2 52.2 %all-gather.3.cloned.1.call-start = ((), (), s32[]{:S(2)}) async-start(), calls=%async_computation.8 | async-start | bytes 2621440 | tf_op jit(solution)/shard_map/all_gather | solution.py:23
  9.3 131.1 %all-gather.5.cloned.1.call-start = ((), (), s32[]{:S(2)}) async-start(), calls=%async_computation.9 | async-start | bytes 14155776 | tf_op jit(solution)/shard_map/all_gather | solution.py:46
  39.1 24.7 %copy-start.2 = (bf16[1152,512]{1,0:T(8,128)(2,1)}, bf16[1152,512]{1,0:T(8,128)(2,1)S(1)}, u32[]{:S(2)}) copy-start(bf16[1152,512]{1,0:T(8,128)(2,1)S(1)} %fusion.1) | copy-start | bytes 3538948
  122.6 33.7 %all-to-all-start = ((bf16[4,128,8]{1,2,0:T(8,128)(2,1)}), bf16[4,128,8]{1,2,0:T(8,128)(2,1)S(1)}, u32[]{:S(2)}, u32[]{:S(2)}) async-start(bf16[4,128,8]{1,2,0:T(8,128)(2,1)} %stack.2), calls=%async_computation | async-start | bytes 16384 | tf_op jit(solution)/shard_map/all_to_all | solution.py:21
  126.0 19.2 %copy-start.7 = (bf16[1,2048,384]{2,1,0:T(8,128)(2,1)S(1)}, bf16[1,2048,384]{2,1,0:T(8,128)(2,1)}, u32[]{:S(2)}) copy-start(bf16[1,2048,384]{2,1,0:T(8,128)(2,1)} %param.12) | copy-start | bytes 4718596
  140.4 5.1 %copy-start.11 = (bf16[2,1152,2048]{2,1,0:T(8,128)(2,1)S(1)}, bf16[2,1152,2048]{2,1,0:T(8,128)(2,1)}, u32[]{:S(2)}) copy-start(bf16[2,1152,2048]{2,1,0:T(8,128)(2,1)} %all-gather.5.cloned.1.call-done) | copy-start | bytes 28311556
  145.5 2.4 copy-start.5
  145.5 2.4 copy-start.12
  147.9 3.9 %copy-start.6 = (f32[1152,384]{0,1:T(8,128)}, f32[1152,384]{0,1:T(8,128)S(1)}, u32[]{:S(2)}) copy-start(f32[1152,384]{0,1:T(8,128)S(1)} %fusion.10) | copy-start | bytes 5308420
  156.2 8.6 %all-to-all-start.4 = ((bf16[4,2,144]{2,1,0:T(2,128)(2,1)}), bf16[4,2,144]{2,1,0:T(2,128)(2,1)S(1)}, u32[]{:S(2)}, u32[]{:S(2)}) async-start(bf16[4,2,144]{2,1,0:T(2,128)(2,1)} %reshape.95), calls=%async_computation.6 | async-start | bytes 8192 | tf_op jit(solution)/shard_map/all_to_all | solution.py:87
  160.1 53.2 %reduce-scatter.4.cloned.1.call-start = ((), (), s32[]{:S(2)}) async-start(), calls=%async_computation.10 | async-start | bytes 14155776 | tf_op jit(solution)/shard_map/reduce_scatter | solution.py:82
  188.4 2.7 copy-start.3
  188.4 2.7 copy-start.8
  217.4 32.1 %all-to-all-start.3 = ((bf16[4,288,1024]{2,1,0:T(8,128)(2,1)}), bf16[4,288,1024]{2,1,0:T(8,128)(2,1)S(1)}, u32[]{:S(2)}, u32[]{:S(2)}) async-start(bf16[4,288,1024]{2,1,0:T(8,128)(2,1)} %bitcast.11), calls=%async_computation.4 | async-start | bytes 4718592 | tf_op jit(solution)/shard_map/all_to_all | solution.py:86
  221.4 49.5 %reduce-scatter.8.cloned.1.call-start = ((), (), s32[]{:S(2)}) async-start(), calls=%async_computation.12 | async-start | bytes 20480 | tf_op jit(solution)/shard_map/reduce_scatter | solution.py:95
  222.0 75.8 %reduce-scatter.6.cloned.1.call-start = ((), (), s32[]{:S(2)}) async-start(), calls=%async_computation.11 | async-start | bytes 2621440 | tf_op jit(solution)/shard_map/reduce_scatter | solution.py:91
  253.6 1.2 copy-start.13
  254.7 12.3 %slice-start = ((s8[9437184]{0:T(1024)(128)(4,1)}), s8[4194304]{0:T(1024)(128)(4,1)S(1)}, s32[]{:S(2)}) async-start(s8[9437184]{0:T(1024)(128)(4,1)} %bitcast.88), calls=%async_computation.13 | async-start | bytes 8388608
  254.7 12.3 %slice-start.1 = ((s8[9437184]{0:T(1024)(128)(4,1)}), s8[4194304]{0:T(1024)(128)(4,1)S(1)}, s32[]{:S(2)}) async-start(s8[9437184]{0:T(1024)(128)(4,1)} %bitcast.88), calls=%async_computation.14 | async-start | bytes 8388608
  260.6 6.4 %copy-start.4 = (bf16[1152,384]{0,1:T(8,128)(2,1)S(1)}, bf16[1152,384]{0,1:T(8,128)(2,1)}, u32[]{:S(2)}) copy-start(bf16[1152,384]{0,1:T(8,128)(2,1)} %copy-done.3) | copy-start | bytes 2654212
  260.6 6.4 %slice-start.2 = ((s8[9437184]{0:T(1024)(128)(4,1)}), s8[1048576]{0:T(1024)(128)(4,1)S(1)}, s32[]{:S(2)}) async-start(s8[9437184]{0:T(1024)(128)(4,1)} %bitcast.88), calls=%async_computation.15 | async-start | bytes 2097152
  267.0 32.5 %copy-start.1 = (bf16[1,2048,384]{2,1,0:T(8,128)(2,1)S(1)}, bf16[1,2048,384]{2,1,0:T(8,128)(2,1)}, u32[]{:S(2)}) copy-start(bf16[1,2048,384]{2,1,0:T(8,128)(2,1)} %param.11) | copy-start | bytes 4718596
  (1 other events, 0.7 us)
Sparse Core Ops, SparseCore 0:
  10.2 49.2 all-gather.2
  121.4 18.9 all-gather.4
  196.4 16.8 reduce-scatter.3
  224.8 20.3 reduce-scatter.7
  253.7 44.0 reduce-scatter.5
